TPU v7x, 512 devices: a whole 4x4x16 slice. The times are simulated.
512 devices in a mesh: tm: 64 (over z, y_hi, core), space: 8 (over y_lo, x).
Axes of the slice: x: 4, y: 4 (y_hi: 2, y_lo: 2; y = y_hi * 2 + y_lo), z: 16, core: 2. Of those that a mesh axis runs over, the one named last changes fastest.
Arguments:
- start_states: float32 [64, 256, 256], P('tm', 'space'), may hold values from -6 to 6
- region_map: int32 [256, 256], P('space'), may hold values from 0 to 3
- source: float32 [2, 256, 256], P(None, 'space'), may hold values from -6 to 6
- front: int32 [], replicated, may hold values from 33 to 63
Outputs:
- new_states: float32 [64, 256, 256], P('tm', 'space')
- jumps: float32 [64, 256, 256], P('tm', 'space')
All inputs are finite; a program needn't handle non-finite values.
Results may differ from a plain program's by a relative error of at most 0.000027.
Values sent between devices are 32-bit elements; how exact they have to be, the bound alone decides.
No kernel may reach another device: no remote copies, remote signals or barrier semaphores. Data moves between devices by JAX's collectives and lax.ppermute only.
A program may use at most 64 MiB of HBM per device.

v0:
```python
import math
import jax
import jax.numpy as jnp
from jax import lax
from jax.sharding import PartitionSpec as P

FINE = 16
ITERS = 2
RELUCTIVITY = (1.0, 0.3, 1.0, 0.25)
SATURATION = (0.0, 2.0, 0.0, 1.5)
MOBILITY = (0.15, 0.02, 0.0004, 0.0008)


def extended_2(block, sides, width):
    for axis, dim in sides:
        count = lax.axis_size(axis)
        forward = [(i, i + 1) for i in range(count - 1)]
        backward = [(target, source) for source, target in forward]
        low = lax.ppermute(
            lax.slice_in_dim(block, block.shape[dim] - width, None, axis=dim), axis, forward
        )
        high = lax.ppermute(lax.slice_in_dim(block, 0, width, axis=dim), axis, backward)
        block = jnp.concatenate([low, block, high], axis=dim)
    return block


def entering(x, axis, combine, identity):
    size, position = (lax.axis_size(axis), lax.axis_index(axis))
    everything = jax.tree.map(lambda part: lax.all_gather(part, axis), x)
    start = jax.tree.map(
        lambda part, zero: jnp.broadcast_to(jnp.asarray(zero, part.dtype), part.shape), x, identity
    )

    def hop(k, before):
        reached = k < position
        new = combine(before, jax.tree.map(lambda part: part[k], everything))
        return jax.tree.map(lambda a, b: jnp.where(reached, a, b), new, before)

    return lax.fori_loop(0, size, hop, start)


def from_root(x, axis, root):
    mine = lax.axis_index(axis) == root
    return lax.psum(jnp.where(mine, x, jnp.zeros_like(x)), axis)


def from_behind(x, axis, by):
    size = lax.axis_size(axis)
    return lax.ppermute(x, axis, [(i, (i + by) % size) for i in range(size)])


def lookup(region_map, table):
    result = jnp.zeros(region_map.shape, jnp.float32)
    for region, entry_value in enumerate(table):
        result = result + jnp.where(
            region_map == region, jnp.float32(entry_value), jnp.float32(0.0)
        )
    return result


def flux_terms(extended, reluctivity, saturation):
    field_cols = jnp.pad(extended, ((0, 0), (1, 1)))
    relu_cols = jnp.pad(reluctivity, ((0, 0), (1, 1)))
    satu_cols = jnp.pad(saturation, ((0, 0), (1, 1)))
    center = field_cols[1:-1, 1:-1]
    own_rel = relu_cols[1:-1, 1:-1]
    own_sat = satu_cols[1:-1, 1:-1]
    divergence = jnp.zeros_like(center)
    diagonal = jnp.zeros_like(center)
    for row_part, col_part in (
        (slice(0, -2), slice(1, -1)),
        (slice(2, None), slice(1, -1)),
        (slice(1, -1), slice(0, -2)),
        (slice(1, -1), slice(2, None)),
    ):
        difference = field_cols[row_part, col_part] - center
        square = difference * difference
        face_rel = 0.5 * (own_rel + relu_cols[row_part, col_part])
        face_sat = 0.5 * (own_sat + satu_cols[row_part, col_part])
        weight = face_rel * (1.0 + face_sat * square / (1.0 + square))
        divergence = divergence + weight * difference
        diagonal = diagonal + weight
    return (divergence, diagonal)


def compose_maps(earlier, later):
    return (later[0] * earlier[0], later[0] * earlier[1] + later[1])


def on_device(start_states, region_map, source, front):
    field_now = start_states[0]
    slices = lax.axis_size("tm")
    slice_index = lax.axis_index("tm")
    scale = 2.0 * math.pi / (slices * FINE)
    stacked = jnp.stack(
        [
            lookup(region_map, RELUCTIVITY),
            lookup(region_map, SATURATION),
            lookup(region_map, MOBILITY),
            source[0],
            source[1],
        ],
        0,
    )
    padded_fields = extended_2(stacked, (("space", 1),), 1)
    mobile = stacked[2]

    def advance(block, values, divergence, step_index):
        phase_angle = (slice_index * FINE + step_index).astype(jnp.float32) * scale
        current = block[3] * jnp.cos(phase_angle) + block[4] * jnp.sin(phase_angle)
        return values + block[2] * (divergence + current)

    def single_step(values, step_index):
        extended = extended_2(values, (("space", 0),), 1)
        divergence, diagonal = flux_terms(extended, padded_fields[0], padded_fields[1])
        return (advance(stacked, values, divergence, step_index), diagonal)

    cut_slice = (front - 1) % slices
    keep_map = slice_index != cut_slice
    fine_end = field_now
    for sweep in range(ITERS):
        fine_values = field_now
        fine_values, fine_diagonal = single_step(fine_values, 0)

        def single_turn(counter, current_values):
            return single_step(current_values, counter)[0]

        fine_values = lax.fori_loop(1, FINE, single_turn, fine_values)
        fine_end = fine_values
        diagonal = fine_diagonal
        decay = 1.0 / (1.0 + FINE * mobile * diagonal)
        decay = jnp.where(keep_map, decay, 0.0)
        offset = fine_end - decay * field_now
        prefix = entering(
            (decay, offset), "tm", compose_maps, (jnp.ones_like(decay), jnp.zeros_like(offset))
        )
        total = compose_maps(prefix, (decay, offset))
        closing = from_root(total[1], "tm", slices - 1)
        field_now = prefix[0] * closing + prefix[1]
    jumps = from_behind(fine_end, "tm", 1) - field_now
    return (field_now[None], jumps[None])


def solution(mesh):
    placed = (P("tm", "space", None), P("space", None), P(None, "space", None), P())
    return jax.shard_map(
        on_device,
        mesh=mesh,
        in_specs=placed,
        out_specs=(P("tm", "space", None), P("tm", "space", None)),
        check_vma=False,
    )
```

profile of v0, /device:TPU:2, one launch (start us, length us, event | category | flops | bytes accessed | tf_op | source)
XLA Modules:
  0.0 1535.7 jit_solution(15619786963016849872)
XLA Ops:
  8.8 3.4 collective-permute-start.4
  12.2 5.7 collective-permute-start.6
  20.5 3.9 collective-permute-start.7
  29.0 142.5 %while.62 = (s32[]{:T(128)}, f32[32,256]{1,0:T(8,128)S(1)}, f32[32,256]{1,0:T(8,128)S(1)}, f32[32,256]{1,0:T(8,128)S(1)}, f32[32,256]{1,0:T(8,128)S(1)}, /*index...) while((s32[]{:T(128)}, f32[32,256]{1,0:T(8,128)S(1)}, ...), condition=%wide.region_1.2_spmd, body=%wide.region_0.1_spmd.sunk | while | flops 520741 | bytes 784917 | solution.py:128
  29.0 3.8 collective-permute-start
  35.0 3.2 collective-permute-done.1
  40.5 3.9 collective-permute-start.1
  48.1 4.6 collective-permute-start.1
  56.2 6.3 collective-permute-start.1
  66.0 6.3 collective-permute-start.1
  75.7 6.3 collective-permute-start.1
  85.5 6.3 collective-permute-start.1
  95.3 6.3 collective-permute-start.1
  105.0 6.3 collective-permute-start.1
  114.8 6.3 collective-permute-start.1
  124.6 6.3 collective-permute-start.1
  134.3 6.3 collective-permute-start.1
  144.1 6.3 collective-permute-start.1
  153.8 6.3 collective-permute-start.1
  163.6 6.3 collective-permute-start.1
  173.0 153.9 %all-gather.9.cloned.1.call-done = f32[2048,256]{1,0:T(8,128)} async-done(((f32[32,256]{1,0:T(8,128)}), f32[2048,256]{1,0:T(8,128)}) %all-gather.9.cloned.1.call-update) | async-done | bytes 2097168 | tf_op jit(solution)/shard_map/all_gather | solution.py:29
  326.9 142.1 %all-gather.11.cloned.1.call-done = f32[2048,256]{1,0:T(8,128)} async-done(((f32[32,256]{1,0:T(8,128)}), f32[2048,256]{1,0:T(8,128)}) %all-gather.11.cloned.1.call-update) | async-done | bytes 2097168 | tf_op jit(solution)/shard_map/all_gather | solution.py:29
  469.0 52.4 %while.64 = (s32[]{:T(128)}, f32[32,256]{1,0:T(8,128)S(1)}, f32[32,256]{1,0:T(8,128)S(1)}, s32[]{:T(128)}, f32[64,32,256]{2,1,0:T(8,128)}, /*index=5*/f32[64,32,256]{2,1,0:T(8,128)}, s32[]{:T(128)}, s32[]{:T(128)}) while((s32[]{:T(128)}, f32[32,256]{1,0:T(8,128)S(1)}, f32[32,256]{1,0:T(8,128)S(1)}, s32[]{:T(128)}, ...), condition=%wide.region_3.4_spmd.clone, body=%wide.region_2.3_spmd.clone.sunk | while | flops 57348 | bytes 196717 | solution.py:39
  522.2 257.2 %psum.14 = f32[32,256]{1,0:T(8,128)S(1)} all-reduce(f32[32,256]{1,0:T(8,128)S(1)} %add_select_fusion.1), channel_id=1, replica_groups=mesh['tm'=64,'space'=8] {'tm'}, use_global_device_ids=true, to_apply=%region_4.5 | all-reduce | flops 8192 | bytes 65536 | tf_op jit(solution)/shard_map/psum | solution.py:44
  779.4 3.4 collective-permute-start.8
  782.7 2.5 collective-permute-start.9
  785.2 3.0 collective-permute-done.9
  788.4 142.2 %while.63 = (s32[]{:T(128)}, f32[32,256]{1,0:T(8,128)S(1)}, f32[32,256]{1,0:T(8,128)S(1)}, f32[32,256]{1,0:T(8,128)S(1)}, f32[32,256]{1,0:T(8,128)S(1)}, /*index...) while((s32[]{:T(128)}, f32[32,256]{1,0:T(8,128)S(1)}, ...), condition=%wide.region_6.7_spmd, body=%wide.region_5.6_spmd.sunk | while | flops 520741 | bytes 784917 | solution.py:128
  788.5 2.5 collective-permute-start.2
  790.9 3.4 collective-permute-start.3
  798.6 3.9 collective-permute-start.3
  806.3 5.7 collective-permute-start.3
  815.4 6.3 collective-permute-start.3
  825.2 6.3 collective-permute-start.3
  835.0 6.3 collective-permute-start.3
  844.7 6.3 collective-permute-start.3
  854.5 6.3 collective-permute-start.3
  864.3 6.3 collective-permute-start.3
  874.0 6.3 collective-permute-start.3
  883.8 6.3 collective-permute-start.3
  893.5 6.3 collective-permute-start.3
  903.3 6.3 collective-permute-start.3
  913.1 6.3 collective-permute-start.3
  922.8 6.3 collective-permute-start.3
  933.9 142.4 %all-gather.13.cloned.1.call-done = f32[2048,256]{1,0:T(8,128)} async-done(((f32[32,256]{1,0:T(8,128)}), f32[2048,256]{1,0:T(8,128)}) %all-gather.13.cloned.1.call-update) | async-done | bytes 2097168 | tf_op jit(solution)/shard_map/all_gather | solution.py:29
  1076.3 141.9 %all-gather.15.cloned.1.call-done = f32[2048,256]{1,0:T(8,128)} async-done(((f32[32,256]{1,0:T(8,128)}), f32[2048,256]{1,0:T(8,128)}) %all-gather.15.cloned.1.call-update) | async-done | bytes 2097168 | tf_op jit(solution)/shard_map/all_gather | solution.py:29
  1218.2 52.4 %while.65 = (s32[]{:T(128)}, f32[32,256]{1,0:T(8,128)S(1)}, f32[32,256]{1,0:T(8,128)S(1)}, s32[]{:T(128)}, f32[64,32,256]{2,1,0:T(8,128)}, /*index=5*/f32[64,32,256]{2,1,0:T(8,128)}, s32[]{:T(128)}, s32[]{:T(128)}) while((s32[]{:T(128)}, f32[32,256]{1,0:T(8,128)S(1)}, f32[32,256]{1,0:T(8,128)S(1)}, s32[]{:T(128)}, ...), condition=%wide.region_8.9_spmd.clone, body=%wide.region_7.8_spmd.clone.sunk | while | flops 57348 | bytes 196717 | solution.py:39
  1271.4 257.2 %psum.15 = f32[32,256]{1,0:T(8,128)S(1)} all-reduce(f32[32,256]{1,0:T(8,128)S(1)} %add_select_fusion), channel_id=1, replica_groups=mesh['tm'=64,'space'=8] {'tm'}, use_global_device_ids=true, to_apply=%region_9.10 | all-reduce | flops 8192 | bytes 65536 | tf_op jit(solution)/shard_map/psum | solution.py:44
  (408 shorter events, 212.4 us)
Async XLA Ops:
  7.2 319.8 %all-gather.9.cloned.1.call-start = ((), (), s32[]{:S(2)}) async-start(), calls=%async_computation | async-start | bytes 2129920 | tf_op jit(solution)/shard_map/all_gather | solution.py:29
  8.8 18.2 %collective-permute-start.4 = (f32[5,1,256]{2,1,0:T(1,128)S(1)}, f32[5,1,256]{2,1,0:T(1,128)S(1)}, u32[]{:S(2)}, u32[]{:S(2)}) collective-permute-start(f32[5,1,256]{2,1,0:T(1,128)S(1)} %get-tuple-element.769), channel_id=1, source_target_pairs={{0,1},{1,2},{2,3},{3,4},{4,5},{5,6},{6,7},{8,9},{9,10},{10,11},{11... | collective-permute-start | bytes 15368 | tf_op jit(solution)/shard_map/ppermute | solution.py:19
  12.2 14.8 collective-permute-start.6
  54.3 8.4 collective-permute-start
  56.2 7.6 collective-permute-start.1
  64.1 8.4 collective-permute-start
  66.0 7.6 collective-permute-start.1
  73.8 8.4 collective-permute-start
  75.7 7.6 collective-permute-start.1
  83.6 8.4 collective-permute-start
  85.5 7.6 collective-permute-start.1
  93.3 8.4 collective-permute-start
  95.3 7.6 collective-permute-start.1
  103.1 8.4 collective-permute-start
  105.0 7.6 collective-permute-start.1
  112.9 8.4 collective-permute-start
  122.6 8.4 collective-permute-start
  124.6 7.6 collective-permute-start.1
  132.4 8.4 collective-permute-start
  134.3 7.6 collective-permute-start.1
  142.2 8.4 collective-permute-start
  144.1 7.6 collective-permute-start.1
  151.9 8.4 collective-permute-start
  153.8 7.6 collective-permute-start.1
  161.7 8.4 collective-permute-start
  163.6 7.6 collective-permute-start.1
  172.2 296.8 %all-gather.11.cloned.1.call-start = ((), (), s32[]{:S(2)}) async-start(), calls=%async_computation.1 | async-start | bytes 2129920 | tf_op jit(solution)/shard_map/all_gather | solution.py:29
  172.9 903.4 %all-gather.13.cloned.1.call-start = ((), (), s32[]{:S(2)}) async-start(), calls=%async_computation.2 | async-start | bytes 2129920 | tf_op jit(solution)/shard_map/all_gather | solution.py:29
  804.3 7.8 collective-permute-start.2
  813.5 8.4 collective-permute-start.2
  823.3 8.4 collective-permute-start.2
  833.0 8.4 collective-permute-start.2
  842.8 8.4 collective-permute-start.2
  852.6 8.4 collective-permute-start.2
  854.5 7.6 collective-permute-start.3
  862.3 8.4 collective-permute-start.2
  864.3 7.6 collective-permute-start.3
  872.1 8.4 collective-permute-start.2
  874.0 7.6 collective-permute-start.3
  881.9 8.4 collective-permute-start.2
  883.8 7.6 collective-permute-start.3
  891.6 8.4 collective-permute-start.2
  893.5 7.6 collective-permute-start.3
  901.4 8.4 collective-permute-start.2
  911.1 8.4 collective-permute-start.2
  920.9 8.4 collective-permute-start.2
  931.4 286.9 %all-gather.15.cloned.1.call-start = ((), (), s32[]{:S(2)}) async-start(), calls=%async_computation.3 | async-start | bytes 2129920 | tf_op jit(solution)/shard_map/all_gather | solution.py:29
  932.0 596.6 %collective-permute-start.10 = (f32[32,256]{1,0:T(8,128)S(1)}, f32[32,256]{1,0:T(8,128)S(1)}, u32[]{:S(2)}, u32[]{:S(2)}) collective-permute-start(f32[32,256]{1,0:T(8,128)S(1)} %get-tuple-element.623), channel_id=1, source_target_pairs={{0,8},{8,16},{16,24},{24,32},{32,40},{40,48},{48,56},{56,64},{64,7... | collective-permute-start | bytes 98312 | tf_op jit(solution)/shard_map/ppermute | solution.py:49
  (25 other events, 909.9 us)
Sparse Core Ops, SparseCore 0:
  172.3 154.6 all-gather.8
  330.8 138.1 all-gather.10
  931.5 144.7 all-gather.12
  1080.0 138.1 all-gather.14
where the time goes:
time: 1550 us; the launch traced here: 1540 us
  waiting for transfers between devices  621 us (40%)
  blocking collectives  514 us (33%)
  starting transfers between devices  257 us (17%)
  other arithmetic  116 us (7%)
    all_gather x4, waiting for transfers between devices, entering(): everything = jax.tree.map(lambda part: lax.all_gather(part, axis), x)  580 us
    psum x2, blocking collectives, from_root(): return lax.psum(jnp.where(mine, x, jnp.zeros_like(x)), axis)  514 us
    ppermute x33, starting transfers between devices, extended_2(): lax.ppermute(lax.slice_in_dim(block, block.shape[dim] - width, None, axis...  183 us
    select_n x128, other arithmetic, hop(): return jax.tree.map(lambda a, b: jnp.where(reached, a, b), new, before)  102 us
    ppermute x33, starting transfers between devices, extended_2(): lax.ppermute(lax.slice_in_dim(block, 0, width, axis=dim), axis, backward)  72.1 us
    ppermute x33, waiting for transfers between devices, extended_2(): lax.ppermute(lax.slice_in_dim(block, block.shape[dim] - width, None, axis...  36.1 us
  transfers between devices with their start and end apart: 71, of which 35 were waited for; matrix products, arithmetic and copies ran while one was open for 4% of the time, Pallas kernels for 0%

commit v1 on v0

--- a/solution.py
+++ b/solution.py
@@ -41,7 +41,7 @@
 
 def from_root(x, axis, root):
     mine = lax.axis_index(axis) == root
-    return lax.psum(jnp.where(mine, x, jnp.zeros_like(x)), axis)
+    return jnp.sum(jax.lax.all_gather(jnp.where(mine, x, jnp.zeros_like(x)), axis), axis=0)
 
 
 def from_behind(x, axis, by):

time: 1550 us -> 1320 us (0.85)
  the two profiles are of different devices: /device:TPU:2 before, /device:TPU:1 now
where the time goes in v1:
time: 1320 us; the launch traced here: 1300 us
  waiting for transfers between devices  921 us (70%)
  starting transfers between devices  235 us (18%)
  other arithmetic  121 us (9%)
  between operations  15.2 us (1%)
    all_gather x4, waiting for transfers between devices, entering(): everything = jax.tree.map(lambda part: lax.all_gather(part, axis), x)  625 us
    all_gather x2, waiting for transfers between devices, from_root(): jax.lax.all_gather(jnp.where(mine, x, jnp.zeros_like(x)), axis)  274 us
    ppermute x33, starting transfers between devices, extended_2(): lax.ppermute(lax.slice_in_dim(block, block.shape[dim] - width, None, axis...  190 us
    select_n x128, other arithmetic, hop(): return jax.tree.map(lambda a, b: jnp.where(reached, a, b), new, before)  102 us
    ppermute x33, starting transfers between devices, extended_2(): lax.ppermute(lax.slice_in_dim(block, 0, width, axis=dim), axis, backward)  42.6 us
  transfers between devices with their start and end apart: 73, of which 38 were waited for; matrix products, arithmetic and copies ran while one was open for 0% of the time, Pallas kernels for 0%

profile of v1, /device:TPU:1, one launch (start us, length us, event | category | flops | bytes accessed | tf_op | source)
XLA Modules:
  0.0 1304.4 jit_solution(5232958034543665809)
XLA Ops:
  8.8 3.9 collective-permute-start.4
  14.8 4.0 collective-permute-start.5
  25.9 125.1 %while.62 = (s32[]{:T(128)}, f32[32,256]{1,0:T(8,128)S(1)}, f32[32,256]{1,0:T(8,128)S(1)}, f32[32,256]{1,0:T(8,128)S(1)}, f32[32,256]{1,0:T(8,128)S(1)}, /*index...) while((s32[]{:T(128)}, f32[32,256]{1,0:T(8,128)S(1)}, ...), condition=%wide.region_1.2_spmd, body=%wide.region_0.1_spmd.sunk | while | flops 520741 | bytes 784917 | solution.py:128
  27.2 4.0 collective-permute-start.1
  33.5 5.1 collective-permute-start.1
  40.9 6.1 collective-permute-start.1
  49.2 6.1 collective-permute-start.1
  57.6 6.3 collective-permute-start.1
  66.2 6.3 collective-permute-start.1
  74.8 6.3 collective-permute-start.1
  83.4 6.3 collective-permute-start.1
  92.1 6.3 collective-permute-start.1
  100.7 6.3 collective-permute-start.1
  109.3 6.3 collective-permute-start.1
  117.9 6.3 collective-permute-start.1
  126.5 6.3 collective-permute-start.1
  135.1 6.3 collective-permute-start.1
  143.8 6.3 collective-permute-start.1
  152.6 175.6 %all-gather.13.cloned.1.call-done = f32[2048,256]{1,0:T(8,128)} async-done(((f32[32,256]{1,0:T(8,128)}), f32[2048,256]{1,0:T(8,128)}) %all-gather.13.cloned.1.call-update) | async-done | bytes 2097168 | tf_op jit(solution)/shard_map/all_gather | solution.py:29
  328.2 142.1 %all-gather.15.cloned.1.call-done = f32[2048,256]{1,0:T(8,128)} async-done(((f32[32,256]{1,0:T(8,128)}), f32[2048,256]{1,0:T(8,128)}) %all-gather.15.cloned.1.call-update) | async-done | bytes 2097168 | tf_op jit(solution)/shard_map/all_gather | solution.py:29
  470.3 52.4 %while.64 = (s32[]{:T(128)}, f32[32,256]{1,0:T(8,128)S(1)}, f32[32,256]{1,0:T(8,128)S(1)}, s32[]{:T(128)}, f32[64,32,256]{2,1,0:T(8,128)}, /*index=5*/f32[64,32,256]{2,1,0:T(8,128)}, s32[]{:T(128)}, s32[]{:T(128)}) while((s32[]{:T(128)}, f32[32,256]{1,0:T(8,128)S(1)}, f32[32,256]{1,0:T(8,128)S(1)}, s32[]{:T(128)}, ...), condition=%wide.region_3.4_spmd.clone, body=%wide.region_2.3_spmd.clone.sunk | while | flops 57348 | bytes 196717 | solution.py:39
  522.6 1.4 add_select_fusion.1
  524.1 138.3 %all-gather.17.cloned.1.call-done = f32[2048,256]{1,0:T(8,128)} async-done(((f32[32,256]{1,0:T(8,128)}), f32[2048,256]{1,0:T(8,128)}) %all-gather.17.cloned.1.call-update) | async-done | bytes 2097168 | tf_op jit(solution)/shard_map/all_gather | solution.py:44
  662.4 1.7 reduce_sum.18
  664.2 3.1 collective-permute-start.8
  668.6 3.0 collective-permute-done.9
  671.8 122.0 %while.63 = (s32[]{:T(128)}, f32[32,256]{1,0:T(8,128)S(1)}, f32[32,256]{1,0:T(8,128)S(1)}, f32[32,256]{1,0:T(8,128)S(1)}, f32[32,256]{1,0:T(8,128)S(1)}, /*index...) while((s32[]{:T(128)}, f32[32,256]{1,0:T(8,128)S(1)}, ...), condition=%wide.region_6.7_spmd, body=%wide.region_5.6_spmd.sunk | while | flops 520741 | bytes 784917 | solution.py:128
  673.2 4.0 collective-permute-start.3
  679.4 4.5 collective-permute-start.3
  686.2 4.2 collective-permute-start.3
  692.7 5.5 collective-permute-start.3
  700.4 6.3 collective-permute-start.3
  709.1 6.3 collective-permute-start.3
  717.7 6.3 collective-permute-start.3
  726.3 6.3 collective-permute-start.3
  734.9 6.3 collective-permute-start.3
  743.5 6.3 collective-permute-start.3
  752.1 6.3 collective-permute-start.3
  760.7 6.3 collective-permute-start.3
  769.4 6.3 collective-permute-start.3
  778.0 6.3 collective-permute-start.3
  786.6 6.3 collective-permute-start.3
  795.3 165.9 %all-gather.19.cloned.1.call-done = f32[2048,256]{1,0:T(8,128)} async-done(((f32[32,256]{1,0:T(8,128)}), f32[2048,256]{1,0:T(8,128)}) %all-gather.19.cloned.1.call-update) | async-done | bytes 2097168 | tf_op jit(solution)/shard_map/all_gather | solution.py:29
  961.1 141.9 %all-gather.21.cloned.1.call-done = f32[2048,256]{1,0:T(8,128)} async-done(((f32[32,256]{1,0:T(8,128)}), f32[2048,256]{1,0:T(8,128)}) %all-gather.21.cloned.1.call-update) | async-done | bytes 2097168 | tf_op jit(solution)/shard_map/all_gather | solution.py:29
  1103.0 52.4 %while.65 = (s32[]{:T(128)}, f32[32,256]{1,0:T(8,128)S(1)}, f32[32,256]{1,0:T(8,128)S(1)}, s32[]{:T(128)}, f32[64,32,256]{2,1,0:T(8,128)}, /*index=5*/f32[64,32,256]{2,1,0:T(8,128)}, s32[]{:T(128)}, s32[]{:T(128)}) while((s32[]{:T(128)}, f32[32,256]{1,0:T(8,128)S(1)}, f32[32,256]{1,0:T(8,128)S(1)}, s32[]{:T(128)}, ...), condition=%wide.region_8.9_spmd.clone, body=%wide.region_7.8_spmd.clone.sunk | while | flops 57348 | bytes 196717 | solution.py:39
  1156.8 2.3 collective-permute-start.10
  1159.1 136.0 %all-gather.23.cloned.1.call-done = f32[2048,256]{1,0:T(8,128)} async-done(((f32[32,256]{1,0:T(8,128)}), f32[2048,256]{1,0:T(8,128)}) %all-gather.23.cloned.1.call-update) | async-done | bytes 2097168 | tf_op jit(solution)/shard_map/all_gather | solution.py:44
  1295.2 1.7 reduce_sum.19
  (414 shorter events, 179.5 us)
Async XLA Ops:
  7.2 321.0 %all-gather.13.cloned.1.call-start = ((), (), s32[]{:S(2)}) async-start(), calls=%async_computation | async-start | bytes 2129920 | tf_op jit(solution)/shard_map/all_gather | solution.py:29
  8.8 15.1 %collective-permute-start.4 = (f32[5,1,256]{2,1,0:T(1,128)S(1)}, f32[5,1,256]{2,1,0:T(1,128)S(1)}, u32[]{:S(2)}, u32[]{:S(2)}) collective-permute-start(f32[5,1,256]{2,1,0:T(1,128)S(1)} %get-tuple-element.769), channel_id=1, source_target_pairs={{0,1},{1,2},{2,3},{3,4},{4,5},{5,6},{6,7},{8,9},{9,10},{10,11},{11... | collective-permute-start | bytes 15368 | tf_op jit(solution)/shard_map/ppermute | solution.py:19
  12.7 11.2 collective-permute-start.6
  39.6 7.6 collective-permute-start
  47.9 7.6 collective-permute-start
  56.3 7.8 collective-permute-start
  57.6 7.1 collective-permute-start.1
  64.9 7.8 collective-permute-start
  66.2 7.1 collective-permute-start.1
  73.5 7.8 collective-permute-start
  74.8 7.1 collective-permute-start.1
  82.1 7.8 collective-permute-start
  83.4 7.1 collective-permute-start.1
  90.8 7.8 collective-permute-start
  92.1 7.1 collective-permute-start.1
  99.4 7.8 collective-permute-start
  100.7 7.1 collective-permute-start.1
  108.0 7.8 collective-permute-start
  116.6 7.8 collective-permute-start
  117.9 7.1 collective-permute-start.1
  125.2 7.8 collective-permute-start
  126.5 7.1 collective-permute-start.1
  133.8 7.8 collective-permute-start
  135.1 7.1 collective-permute-start.1
  142.5 7.8 collective-permute-start
  143.8 7.1 collective-permute-start.1
  151.8 318.5 %all-gather.15.cloned.1.call-start = ((), (), s32[]{:S(2)}) async-start(), calls=%async_computation.1 | async-start | bytes 2129920 | tf_op jit(solution)/shard_map/all_gather | solution.py:29
  152.5 509.9 %all-gather.17.cloned.1.call-start = ((), (), s32[]{:S(2)}) async-start(), calls=%async_computation.2 | async-start | bytes 2129920 | tf_op jit(solution)/shard_map/all_gather | solution.py:44
  524.1 437.1 %all-gather.19.cloned.1.call-start = ((), (), s32[]{:S(2)}) async-start(), calls=%async_computation.3 | async-start | bytes 2129920 | tf_op jit(solution)/shard_map/all_gather | solution.py:29
  699.1 7.8 collective-permute-start.2
  700.4 7.1 collective-permute-start.3
  707.8 7.8 collective-permute-start.2
  709.1 7.1 collective-permute-start.3
  716.4 7.8 collective-permute-start.2
  717.7 7.1 collective-permute-start.3
  725.0 7.8 collective-permute-start.2
  726.3 7.1 collective-permute-start.3
  733.6 7.8 collective-permute-start.2
  734.9 7.1 collective-permute-start.3
  742.2 7.8 collective-permute-start.2
  750.8 7.8 collective-permute-start.2
  759.4 7.8 collective-permute-start.2
  768.1 7.8 collective-permute-start.2
  776.7 7.8 collective-permute-start.2
  785.3 7.8 collective-permute-start.2
  794.6 308.4 %all-gather.21.cloned.1.call-start = ((), (), s32[]{:S(2)}) async-start(), calls=%async_computation.4 | async-start | bytes 2129920 | tf_op jit(solution)/shard_map/all_gather | solution.py:29
  795.2 500.0 %all-gather.23.cloned.1.call-start = ((), (), s32[]{:S(2)}) async-start(), calls=%async_computation.5 | async-start | bytes 2129920 | tf_op jit(solution)/shard_map/all_gather | solution.py:44
  1156.8 140.1 %collective-permute-start.10 = (f32[32,256]{1,0:T(8,128)S(1)}, f32[32,256]{1,0:T(8,128)S(1)}, u32[]{:S(2)}, u32[]{:S(2)}) collective-permute-start(f32[32,256]{1,0:T(8,128)S(1)} %get-tuple-element.623), channel_id=1, source_target_pairs={{0,8},{8,16},{16,24},{24,32},{32,40},{40,48},{48,56},{56,64},{64,7... | collective-permute-start | bytes 98312 | tf_op jit(solution)/shard_map/ppermute | solution.py:49
  (27 other events, 796.4 us)
Sparse Core Ops, SparseCore 0:
  151.9 176.2 all-gather.12
  332.1 138.1 all-gather.14
  524.2 138.1 all-gather.16
  794.7 166.3 all-gather.18
  964.8 138.1 all-gather.20
  1157.0 138.1 all-gather.22
